TPU v7x, 256 devices: a whole 4x4x8 slice. The times are simulated.
256 devices in a mesh: ctx: 32 (over x, z_lo, y), head: 8 (over z_hi, core).
Axes of the slice: x: 4, y: 4, z: 8 (z_hi: 4, z_lo: 2; z = z_hi * 2 + z_lo), core: 2. Of those that a mesh axis runs over, the one named last changes fastest.
Arguments:
- tokens: bfloat16 [8192, 4096], P('ctx', 'head'), may hold values from -6 to 6
- cotangent: bfloat16 [8192, 4096], P('ctx', 'head'), may hold values from -0.1796875 to 0.1796875
- expert_ids: int32 [8192, 2], P('ctx'), may hold values from 0 to 31, all different within a row; in each aligned block of 256 rows (0 to 255, 256 to 511, ...) at most 24 rows name the same one
- w_router: bfloat16 [4096, 32], P('head'), may hold values from -0.09375 to 0.09375
- w_gate: bfloat16 [32, 1408, 4096], P('ctx', None, 'head'), may hold values from -0.09375 to 0.09375
- w_up: bfloat16 [32, 1408, 4096], P('ctx', None, 'head'), may hold values from -0.09375 to 0.09375
- w_down: bfloat16 [32, 1408, 4096], P('ctx', None, 'head'), may hold values from -0.15625 to 0.15625
Outputs:
- mixed: bfloat16 [8192, 4096], P('ctx', 'head')
- grad_tokens: bfloat16 [8192, 4096], P('ctx', 'head')
- grad_router: float32 [4096, 32], P('head')
- grad_gate: bfloat16 [32, 1408, 4096], P('ctx', None, 'head')
- grad_up: bfloat16 [32, 1408, 4096], P('ctx', None, 'head')
- grad_down: bfloat16 [32, 1408, 4096], P('ctx', None, 'head')
Inputs may be any that keep to these rules, and one draw needn't show every extreme that they name: `expert_ids`: each row names 2 different experts. Within the rows of one device (aligned blocks of 256 rows) no expert is named by more than 24 rows, a bound that some block reaches.
All inputs are finite; a program needn't handle non-finite values.
Results may differ from a plain program's by a relative error of at most 0.023.
Values may be sent and summed in bfloat16 or wider, within the bound.
No kernel may reach another device: no remote copies, remote signals or barrier semaphores. Data moves between devices by JAX's collectives and lax.ppermute only.
A program may use at most 64 MiB of HBM per device.

v0:
```python
import jax
import jax.numpy as jnp
from jax import lax
from jax.sharding import PartitionSpec as P


def contract_rows(left, right):
    return lax.dot_general(
        left, right, (((0,), (0,)), ((), ())), preferred_element_type=jnp.float32
    )


def contract_last(left, right):
    return lax.dot_general(
        left, right, (((1,), (1,)), ((), ())), preferred_element_type=jnp.float32
    )


def activations(gate_pre, up_pre, back_proj, prob_rows):
    sigma = jax.nn.sigmoid(gate_pre)
    active = gate_pre * sigma
    hidden = (active * up_pre).astype(jnp.bfloat16)
    hidden_grad = prob_rows[:, None] * back_proj
    gate_grad = (hidden_grad * up_pre * sigma * (1.0 + gate_pre * (1.0 - sigma))).astype(
        jnp.bfloat16
    )
    up_grad = (hidden_grad * active).astype(jnp.bfloat16)
    return (hidden, gate_grad, up_grad)


def local(tokens, cotangent, expert_ids, w_router, w_gate, w_up, w_down):
    ctx_count = lax.axis_size("ctx")
    tok_rows = tokens.shape[0]
    shard_width = tokens.shape[1]
    pick_count = expert_ids.shape[1]
    experts = w_router.shape[1]
    capacity = 3 * tok_rows * pick_count // (2 * experts)
    partial_logits = jnp.dot(tokens, w_router, preferred_element_type=jnp.float32)
    onehot = (expert_ids[:, :, None] == jnp.arange(experts, dtype=jnp.int32)[None, None, :]).astype(
        jnp.float32
    )
    chosen = lax.psum(jnp.sum(partial_logits[:, None, :] * onehot, axis=2), "head")
    prob_pairs = jnp.stack(
        [jax.nn.sigmoid(chosen[:, 0] - chosen[:, 1]), jax.nn.sigmoid(chosen[:, 1] - chosen[:, 0])],
        axis=1,
    )
    flat_ids = expert_ids.reshape(-1)
    id_hits = (flat_ids[:, None] == jnp.arange(experts, dtype=jnp.int32)[None, :]).astype(jnp.int32)
    places = jnp.sum((jnp.cumsum(id_hits, axis=0) - 1) * id_hits, axis=1)
    slot_index = flat_ids * capacity + places
    slot_table = (
        jnp.zeros((experts * capacity,), jnp.int32)
        .at[slot_index]
        .set(jnp.arange(tok_rows * pick_count, dtype=jnp.int32) + 1)
    )
    occupied = slot_table > 0
    source = jnp.maximum(slot_table - 1, 0)
    row_index = source // pick_count
    prob_send = jnp.where(occupied, prob_pairs.reshape(-1)[source], jnp.float32(0.0)).reshape(
        experts, capacity
    )

    def pack_rows(values):
        picked = jnp.where(occupied[:, None], values[row_index], jnp.zeros((), values.dtype))
        return picked.reshape(experts, capacity, values.shape[1])

    recv_x, recv_g, recv_p = (
        lax.all_to_all(pack_rows(tokens), "ctx", split_axis=0, concat_axis=0, tiled=True),
        lax.all_to_all(pack_rows(cotangent), "ctx", split_axis=0, concat_axis=0, tiled=True),
        lax.all_to_all(
            prob_send.astype(jnp.bfloat16), "ctx", split_axis=0, concat_axis=0, tiled=True
        ).astype(prob_send.dtype),
    )
    slot_count = recv_x.shape[0] * recv_x.shape[1]
    x_rows = recv_x.reshape(slot_count, shard_width)
    cot_rows = recv_g.reshape(slot_count, shard_width)
    prob_rows = recv_p.reshape(slot_count)
    gate_w = w_gate[0]
    up_w = w_up[0]
    down_w = w_down[0]
    gate_part = contract_last(x_rows, gate_w)
    up_part = contract_last(x_rows, up_w)
    back_part = contract_last(cot_rows, down_w)
    gate_pre, up_pre, back_proj = (
        lax.psum(gate_part.astype(jnp.bfloat16), "head").astype(jnp.float32),
        lax.psum(up_part.astype(jnp.bfloat16), "head").astype(jnp.float32),
        lax.psum(back_part.astype(jnp.bfloat16), "head").astype(jnp.float32),
    )
    hidden, gate_grad, up_grad = activations(gate_pre, up_pre, back_proj, prob_rows)
    out_rows = jnp.dot(hidden, down_w, preferred_element_type=jnp.float32).astype(jnp.bfloat16)
    dx_rows = (
        jnp.dot(gate_grad, gate_w, preferred_element_type=jnp.float32)
        + jnp.dot(up_grad, up_w, preferred_element_type=jnp.float32)
    ).astype(jnp.bfloat16)
    hidden_kept = lax.optimization_barrier(hidden)
    scaled = (prob_rows[:, None] * hidden_kept.astype(jnp.float32)).astype(jnp.bfloat16)
    grad_down = contract_rows(scaled, cot_rows).astype(jnp.bfloat16)[None]
    grad_gate = contract_rows(gate_grad, x_rows).astype(jnp.bfloat16)[None]
    grad_up = contract_rows(up_grad, x_rows).astype(jnp.bfloat16)[None]
    back_out, back_dx = (
        lax.all_to_all(
            out_rows.reshape(ctx_count, capacity, shard_width),
            "ctx",
            split_axis=0,
            concat_axis=0,
            tiled=True,
        ),
        lax.all_to_all(
            dx_rows.reshape(ctx_count, capacity, shard_width),
            "ctx",
            split_axis=0,
            concat_axis=0,
            tiled=True,
        ),
    )
    out_pairs = back_out.reshape(experts * capacity, shard_width)[slot_index].reshape(
        tok_rows, pick_count, shard_width
    )
    dx_pairs = back_dx.reshape(experts * capacity, shard_width)[slot_index].reshape(
        tok_rows, pick_count, shard_width
    )
    mixed = jnp.sum(prob_pairs[:, :, None] * out_pairs.astype(jnp.float32), axis=1).astype(
        jnp.bfloat16
    )
    score_part = jnp.sum(
        cotangent.astype(jnp.float32)[:, None, :] * out_pairs.astype(jnp.float32), axis=2
    )
    score_grad = lax.psum(score_part, "head")
    logit_lead = prob_pairs[:, 0] * prob_pairs[:, 1] * (score_grad[:, 0] - score_grad[:, 1])
    logit_grad = jnp.stack([logit_lead, -logit_lead], axis=1)
    dense_grad = jnp.sum(logit_grad[:, :, None] * onehot, axis=1)
    router_term = jnp.dot(
        dense_grad, w_router.astype(jnp.float32).T, precision=lax.Precision.HIGHEST
    )
    grad_tokens = (
        dx_pairs[:, 0].astype(jnp.float32) + dx_pairs[:, 1].astype(jnp.float32) + router_term
    ).astype(jnp.bfloat16)
    router_part = jnp.dot(tokens.astype(jnp.float32).T, dense_grad, precision=lax.Precision.HIGHEST)
    grad_router = lax.psum(router_part, "ctx")
    return (mixed, grad_tokens, grad_router, grad_gate, grad_up, grad_down)


def solution(mesh):
    placed = (
        P("ctx", "head"),
        P("ctx", "head"),
        P("ctx", None),
        P("head", None),
        P("ctx", None, "head"),
        P("ctx", None, "head"),
        P("ctx", None, "head"),
    )
    return jax.shard_map(
        local,
        mesh=mesh,
        in_specs=placed,
        out_specs=(
            P("ctx", "head"),
            P("ctx", "head"),
            P("head", None),
            P("ctx", None, "head"),
            P("ctx", None, "head"),
            P("ctx", None, "head"),
        ),
        check_vma=False,
    )
```

profile of v0, /device:TPU:64, one launch (start us, length us, event | category | flops | bytes accessed | tf_op | source)
XLA Modules:
  0.0 605.1 jit_solution(14181950294091375107)
XLA Ops:
  7.2 0.0 copy-start
  7.2 0.9 copy.53
  8.1 0.1 eq.45
  8.3 0.1 eq.41
  8.4 0.7 broadcast_multiply_fusion
  9.1 1.2 reduce-window.6
  10.3 0.2 slice_reduce_fusion
  10.6 0.1 copy.52
  10.7 0.1 mul.105
  10.9 0.1 fusion.28
  11.0 2.4 scatter_custom_fusion
  13.5 1.1 fusion.37
  14.6 0.7 select_reduce_fusion.1
  15.3 15.2 %psum.42 = f32[256,2]{0,1:T(2,128)S(1)} all-reduce(f32[256,2]{0,1:T(2,128)S(1)} %select_reduce_fusion.1), channel_id=1, replica_groups=mesh['ctx'=32,'head'=8] {'head'}, use_global_device_ids=true, to_apply=%region_1.0 | all-reduce | flops 512 | bytes 4096 | tf_op jit(solution)/shard_map/psum | solution.py:42
  30.6 0.1 copy.51
  30.7 0.1 reshape.144
  30.9 5.0 gather_fusion.2
  35.9 0.6 select_convert_fusion
  36.5 0.1 broadcast_in_dim.50
  36.6 2.7 gather_fusion
  39.3 2.7 gather_fusion.3
  42.0 1.1 broadcast_select_fusion
  43.1 20.9 %all_to_all.26 = bf16[32,24,512]{2,1,0:T(8,128)(2,1)S(1)} all-to-all(bf16[32,24,512]{2,1,0:T(8,128)(2,1)S(1)} %get-tuple-element.21), channel_id=1, replica_groups=mesh['ctx'=32,'head'=8] {'ctx'}, dimensions={0} | all-to-all | bytes 1572864 | tf_op jit(solution)/shard_map/all_to_all | solution.py:68
  64.0 4.4 all-to-all-start.3
  68.4 0.0 all-reduce.6.cloned.1.call-start
  68.4 2.8 convolution_convert_fusion.1
  71.2 2.8 convolution_convert_fusion.2
  74.0 6.5 %all-to-all-done.3 = bf16[32,24,512]{2,1,0:T(8,128)(2,1)S(1)} async-done(((bf16[32,24,512]{2,1,0:T(8,128)(2,1)}), bf16[32,24,512]{2,1,0:T(8,128)(2,1)S(1)}, u32[]{:S(2)}, u32[]{:S(2)}) %all-to-all-start.3) | async-done | bytes 786464 | tf_op jit(solution)/shard_map/all_to_all | solution.py:69
  80.6 4.4 convolution_convert_fusion
  85.0 0.0 all-reduce.6.cloned.1.call-update
  85.0 0.7 copy-done.16
  85.7 0.1 convert_element_type.137
  85.8 12.5 %all_to_all.27 = bf16[32,1,24]{2,1,0:T(2,128)(2,1)S(1)} all-to-all(bf16[32,1,24]{2,1,0:T(2,128)(2,1)S(1)} %convert_element_type.137), channel_id=1, replica_groups=mesh['ctx'=32,'head'=8] {'ctx'}, dimensions={0} | all-to-all | bytes 3072 | tf_op jit(solution)/shard_map/all_to_all | solution.py:70
  98.3 0.1 convert_reduce_fusion
  98.3 0.1 reshape.150
  98.4 137.6 %all-reduce.6.cloned.1.call-done = (bf16[768,1408]{1,0:T(8,128)(2,1)}, bf16[768,1408]{1,0:T(8,128)(2,1)}, bf16[768,1408]{1,0:T(8,128)(2,1)}) async-done(((bf16[768,1408]{1,0:T(8,128)(2,1)}, bf16[768,1408]{1,0:T(8,128)(2,1)}, bf16[768,1408]{1,0:T(8,128)(2,1)}), (bf16[768,1408]{1,0:T(8,128)(2,1)}, bf16[768,1408]{1,0:T(8,128)(2,1)}, bf16[768,1408]{1,0:T(8,128)(2,1)})) %all-reduce.6.cloned.1.call-update) | async-done | bytes 6488080 | tf_op jit(solution)/shard_map/psum | solution.py:86
  236.0 6.0 fusion.3
  242.1 1.4 fusion.15
  243.5 0.7 copy-done.6
  244.1 0.3 copy-done.18
  244.5 2.3 add_convert_fusion
  246.7 8.4 %all-to-all-start.4 = ((bf16[32,24,512]{2,1,0:T(8,128)(2,1)}), bf16[32,24,512]{2,1,0:T(8,128)(2,1)S(1)}, u32[]{:S(2)}, u32[]{:S(2)}) async-start(bf16[32,24,512]{2,1,0:T(8,128)(2,1)} %bitcast.12), calls=%async_computation.4 | async-start | bytes 1572864 | tf_op jit(solution)/shard_map/all_to_all | solution.py:108
  255.2 4.3 fusion.21
  259.5 8.7 %all-to-all-done.4 = bf16[32,24,512]{2,1,0:T(8,128)(2,1)S(1)} async-done(((bf16[32,24,512]{2,1,0:T(8,128)(2,1)}), bf16[32,24,512]{2,1,0:T(8,128)(2,1)S(1)}, u32[]{:S(2)}, u32[]{:S(2)}) %all-to-all-start.4) | async-done | bytes 786464 | tf_op jit(solution)/shard_map/all_to_all | solution.py:108
  268.1 4.8 all-to-all-start.1
  273.0 0.0 all-reduce.4.cloned.1.call-start
  273.0 0.9 convert_element_type.128
  273.9 0.7 pad_clamp_fusion.1
  274.6 4.3 fusion.8
  279.0 2.4 fusion.9
  281.4 2.5 fusion.10
  283.9 2.6 gather_fusion.4
  286.5 1.2 reshape.148
  287.8 1.7 fusion.36
  289.5 2.6 gather_fusion.1
  292.1 1.8 reshape.149
  293.9 3.8 multiply_reduce_fusion
  297.7 0.1 copy.60
  297.8 15.7 %psum.46 = f32[256,2]{0,1:T(2,128)S(1)} all-reduce(f32[256,2]{0,1:T(2,128)S(1)} %copy.60), channel_id=1, replica_groups=mesh['ctx'=32,'head'=8] {'head'}, use_global_device_ids=true, to_apply=%region_11.12 | all-reduce | flops 512 | bytes 4096 | tf_op jit(solution)/shard_map/psum | solution.py:128
  313.5 0.9 convolution_bitcast_fusion
  314.4 0.0 all-reduce.4.cloned.1.call-update
  314.4 2.2 fusion.26
  316.6 280.1 %all-reduce.4.cloned.1.call-done = f32[512,32]{0,1:T(8,128)} async-done(((f32[512,32]{0,1:T(8,128)}), f32[512,32]{0,1:T(8,128)}) %all-reduce.4.cloned.1.call-update) | async-done | bytes 65552 | tf_op jit(solution)/shard_map/psum | solution.py:139
  596.8 1.5 copy.71
  (47 shorter events, 0.2 us)
Async XLA Ops:
  7.2 61.2 %copy-start = (bf16[1,1408,512]{2,1,0:T(8,128)(2,1)S(1)}, bf16[1,1408,512]{2,1,0:T(8,128)(2,1)}, u32[]{:S(2)}) copy-start(bf16[1,1408,512]{2,1,0:T(8,128)(2,1)} %param.12) | copy-start | bytes 4325380
  7.2 29.4 %copy-start.1 = (bf16[256,512]{1,0:T(8,128)(2,1)S(1)}, bf16[256,512]{1,0:T(8,128)(2,1)}, u32[]{:S(2)}) copy-start(bf16[256,512]{1,0:T(8,128)(2,1)} %param.7) | copy-start | bytes 786436
  11.0 19.9 %copy-start.15 = (s32[512,1]{0,1:T(1,128)}, s32[512,1]{0,1:T(1,128)S(1)}, u32[]{:S(2)}) copy-start(s32[512,1]{0,1:T(1,128)S(1)} %compare_select_fusion) | copy-start | bytes 6148
  30.7 5.9 copy-start.7
  36.6 2.7 copy-start.2
  64.0 7.2 %copy-start.9 = (bf16[32,24,512]{2,1,0:T(8,128)(2,1)}, bf16[32,24,512]{2,1,0:T(8,128)(2,1)S(1)}, u32[]{:S(2)}) copy-start(bf16[32,24,512]{2,1,0:T(8,128)(2,1)S(1)} %all_to_all.26) | copy-start | bytes 2359300
  64.0 16.6 %all-to-all-start.3 = ((bf16[32,24,512]{2,1,0:T(8,128)(2,1)}), bf16[32,24,512]{2,1,0:T(8,128)(2,1)S(1)}, u32[]{:S(2)}, u32[]{:S(2)}) async-start(bf16[32,24,512]{2,1,0:T(8,128)(2,1)} %get-tuple-element.20), calls=%async_computation.3 | async-start | bytes 1572864 | tf_op jit(solution)/shard_map/all_to_all | solution.py:69
  68.4 167.7 %all-reduce.6.cloned.1.call-start = ((), (), s32[]{:S(2)}) async-start(), calls=%async_computation.6 | async-start | bytes 12976128 | tf_op jit(solution)/shard_map/psum | solution.py:86
  68.4 2.8 copy-start.17
  80.6 4.4 copy-start.11
  85.0 0.7 copy-start.16
  242.1 1.4 copy-start.4
  242.1 2.1 copy-start.6
  242.1 2.4 copy-start.18
  246.7 21.4 %all-to-all-start.4 = ((bf16[32,24,512]{2,1,0:T(8,128)(2,1)}), bf16[32,24,512]{2,1,0:T(8,128)(2,1)S(1)}, u32[]{:S(2)}, u32[]{:S(2)}) async-start(bf16[32,24,512]{2,1,0:T(8,128)(2,1)} %bitcast.12), calls=%async_computation.4 | async-start | bytes 1572864 | tf_op jit(solution)/shard_map/all_to_all | solution.py:108
  268.1 21.3 %all-to-all-start.1 = ((bf16[32,24,512]{2,1,0:T(8,128)(2,1)}), bf16[32,24,512]{2,1,0:T(8,128)(2,1)S(1)}, u32[]{:S(2)}, u32[]{:S(2)}) async-start(bf16[32,24,512]{2,1,0:T(8,128)(2,1)} %bitcast.81), calls=%async_computation.1 | async-start | bytes 1572864 | tf_op jit(solution)/shard_map/all_to_all | solution.py:101
  273.0 323.8 %all-reduce.4.cloned.1.call-start = ((), (), s32[]{:S(2)}) async-start(), calls=%async_computation.5 | async-start | bytes 131072 | tf_op jit(solution)/shard_map/psum | solution.py:139
  274.6 4.4 copy-start.5
  274.6 4.4 copy-start.10
  278.9 2.4 copy-start.3
  278.9 2.4 copy-start.12
  292.1 21.4 %copy-start.14 = (s32[256,2]{0,1:T(2,128)S(1)}, s32[256,2]{0,1:T(2,128)}, u32[]{:S(2)}) copy-start(s32[256,2]{0,1:T(2,128)} %param.9) | copy-start | bytes 6148
  292.1 22.3 %copy-start.8 = (bf16[256,1,512]{2,1,0:T(2,128)(2,1)S(1)}, bf16[256,1,512]{2,1,0:T(2,128)(2,1)}, u32[]{:S(2)}) copy-start(bf16[256,1,512]{2,1,0:T(2,128)(2,1)} %get-tuple-element.18) | copy-start | bytes 786436
  292.1 22.3 %copy-start.13 = (bf16[512,32]{0,1:T(8,128)(2,1)S(1)}, bf16[512,32]{0,1:T(8,128)(2,1)}, u32[]{:S(2)}) copy-start(bf16[512,32]{0,1:T(8,128)(2,1)} %param.10) | copy-start | bytes 98308
Sparse Core Ops, SparseCore 0:
  85.1 150.8 all-reduce.5
  314.5 282.1 all-reduce.3
where the time goes:
time: 606 us; the launch traced here: 605 us
  waiting for transfers between devices  433 us (71%)
  blocking collectives  64.3 us (11%)
  matrix products  31.5 us (5%)
  local copies, waits for them, and re-layouts  28.3 us (5%)
  starting transfers between devices  17.7 us (3%)
  other arithmetic  15.9 us (3%)
  between operations  14.4 us (2%)
    psum x1, waiting for transfers between devices, local(): grad_router = lax.psum(router_part, 'ctx')  280 us
    psum x1, waiting for transfers between devices, local(): lax.psum(up_part.astype(jnp.bfloat16), 'head').astype(jnp.float32)  138 us
    all_to_all x1, blocking collectives, local(): lax.all_to_all(pack_rows(tokens), 'ctx', split_axis=0, concat_axis=0, til...  20.9 us
    psum x1, blocking collectives, local(): score_grad = lax.psum(score_part, 'head')  15.7 us
    psum x1, blocking collectives, local(): lax.psum(jnp.sum(partial_logits[:, None, :] * onehot, axis=2), 'head')  15.2 us
    all_to_all x1, blocking collectives, local(): lax.all_to_all(prob_send.astype(jnp.bfloat16), 'ctx', split_axis=0, conca...  12.5 us
  transfers between devices with their start and end apart: 5, of which 4 were waited for; matrix products, arithmetic and copies ran while one was open for 5% of the time, Pallas kernels for 0%

commit v1 on v0

--- a/solution.py
+++ b/solution.py
@@ -81,9 +81,10 @@
     gate_part = contract_last(x_rows, gate_w)
     up_part = contract_last(x_rows, up_w)
     back_part = contract_last(cot_rows, down_w)
+    cubes_choose = lambda obj, a_name: lax.all_gather(obj, a_name).sum(axis=0)
     gate_pre, up_pre, back_proj = (
         lax.psum(gate_part.astype(jnp.bfloat16), "head").astype(jnp.float32),
-        lax.psum(up_part.astype(jnp.bfloat16), "head").astype(jnp.float32),
+        cubes_choose(up_part.astype(jnp.bfloat16), "head").astype(jnp.float32),
         lax.psum(back_part.astype(jnp.bfloat16), "head").astype(jnp.float32),
     )
     hidden, gate_grad, up_grad = activations(gate_pre, up_pre, back_proj, prob_rows)

time: 606 us -> 718 us (1.18)
  waiting for transfers between devices: 433 us -> 534 us
  other arithmetic: 15.9 us -> 27.9 us
    all_gather x0 -> x1, waiting for transfers between devices: none -> 127 us  [local(): cubes_choose = lambda obj, a_name: lax.all_gather(obj, a_name).sum(axis=0)]
    psum x1, waiting for transfers between devices: 138 us -> 110 us  [local(): lax.psum(gate_part.astype(jnp.bfloat16), 'head').astype(jnp.float32)]
    reduce_sum x0 -> x1, other arithmetic: none -> 10.7 us  [local(): cubes_choose = lambda obj, a_name: lax.all_gather(obj, a_name).sum(axis=0)]
    all_to_all x1, waiting for transfers between devices: 8.67 us -> 0.01 us  [local(): lax.all_to_all(dx_rows.reshape(ctx_count, capacity, shard_width), 'ctx',...]
  transfers between devices with their start and end apart: 5 -> 6, of which waited for: 4 -> 5; matrix products, arithmetic and copies ran while one was open for 5% -> 6% of each run, Pallas kernels for 0% -> 0%
where the time goes in v1:
time: 718 us; the launch traced here: 717 us
  waiting for transfers between devices  534 us (74%)
  blocking collectives  63.8 us (9%)
  matrix products  30.1 us (4%)
  local copies, waits for them, and re-layouts  29.9 us (4%)
  other arithmetic  27.9 us (4%)
  starting transfers between devices  16.7 us (2%)
  between operations  14.1 us (2%)
    psum x1, waiting for transfers between devices, local(): grad_router = lax.psum(router_part, 'ctx')  283 us
    all_gather x1, waiting for transfers between devices, local(): cubes_choose = lambda obj, a_name: lax.all_gather(obj, a_name).sum(axis=0)  127 us
    psum x1, waiting for transfers between devices, local(): lax.psum(gate_part.astype(jnp.bfloat16), 'head').astype(jnp.float32)  110 us
    all_to_all x1, blocking collectives, local(): lax.all_to_all(pack_rows(tokens), 'ctx', split_axis=0, concat_axis=0, til...  20.9 us
    psum x1, blocking collectives, local(): lax.psum(jnp.sum(partial_logits[:, None, :] * onehot, axis=2), 'head')  15.8 us
  transfers between devices with their start and end apart: 6, of which 5 were waited for; matrix products, arithmetic and copies ran while one was open for 6% of the time, Pallas kernels for 0%

profile of v1, /device:TPU:64, one launch (start us, length us, event | category | flops | bytes accessed | tf_op | source)
XLA Modules:
  0.0 717.0 jit_solution(14111129826106009604)
XLA Ops:
  7.2 0.0 all-gather.3.cloned.1.call-start
  7.2 0.8 broadcast_multiply_fusion
  8.1 0.8 copy.53
  8.9 0.1 eq.41
  9.0 0.1 eq.45
  9.2 0.1 copy.52
  9.3 0.1 mul.105
  9.5 1.2 reduce-window.6
  10.6 0.2 slice_reduce_fusion
  10.9 0.1 fusion.28
  11.0 2.4 scatter_custom_fusion
  13.6 2.7 gather_fusion.3
  16.3 2.7 gather_fusion
  19.0 0.9 fusion.37
  19.9 0.0 copy-done.13
  19.9 15.8 %psum.35 = f32[256,2]{0,1:T(2,128)} all-reduce(f32[256,2]{0,1:T(2,128)S(1)} %select_reduce_fusion.1), channel_id=1, replica_groups=mesh['ctx'=32,'head'=8] {'head'}, use_global_device_ids=true, to_apply=%region_1.0 | all-reduce | flops 512 | bytes 4096 | tf_op jit(solution)/shard_map/psum | solution.py:42
  35.7 0.8 add_divide_fusion.1
  36.5 0.5 copy-done.16
  37.1 0.6 pad_maximum_fusion
  37.6 1.5 copy.51
  39.1 1.0 reshape.144
  40.2 6.7 gather_fusion.2
  46.9 1.2 select_convert_fusion
  48.1 0.8 broadcast_in_dim.50
  48.9 1.1 broadcast_select_fusion
  50.0 20.9 %all_to_all.26 = bf16[32,24,512]{2,1,0:T(8,128)(2,1)S(1)} all-to-all(bf16[32,24,512]{2,1,0:T(8,128)(2,1)S(1)} %get-tuple-element.20), channel_id=1, replica_groups=mesh['ctx'=32,'head'=8] {'ctx'}, dimensions={0} | all-to-all | bytes 1572864 | tf_op jit(solution)/shard_map/all_to_all | solution.py:68
  70.9 2.8 convolution_convert_fusion.1
  73.7 4.4 all-to-all-start.3
  78.1 0.0 all-reduce.6.cloned.1.call-start
  78.2 4.2 convolution_convert_fusion.2
  82.4 8.0 %all-to-all-done.3 = bf16[32,24,512]{2,1,0:T(8,128)(2,1)S(1)} async-done(((bf16[32,24,512]{2,1,0:T(8,128)(2,1)}), bf16[32,24,512]{2,1,0:T(8,128)(2,1)S(1)}, u32[]{:S(2)}, u32[]{:S(2)}) %all-to-all-start.3) | async-done | bytes 786464 | tf_op jit(solution)/shard_map/all_to_all | solution.py:69
  90.3 2.8 convolution_convert_fusion
  93.1 0.0 all-reduce.6.cloned.1.call-update
  93.1 0.1 convert_element_type.139
  93.2 13.2 %all_to_all.27 = bf16[32,1,24]{2,1,0:T(2,128)(2,1)S(1)} all-to-all(bf16[32,1,24]{2,1,0:T(2,128)(2,1)S(1)} %convert_element_type.139), channel_id=1, replica_groups=mesh['ctx'=32,'head'=8] {'ctx'}, dimensions={0} | all-to-all | bytes 3072 | tf_op jit(solution)/shard_map/all_to_all | solution.py:70
  106.5 0.1 convert_reduce_fusion
  106.5 0.1 reshape.150
  106.6 127.2 %all-gather.3.cloned.1.call-done = bf16[6144,1408]{1,0:T(8,128)(2,1)} async-done(((bf16[768,1408]{1,0:T(8,128)(2,1)}), bf16[6144,1408]{1,0:T(8,128)(2,1)}) %all-gather.3.cloned.1.call-update) | async-done | bytes 17301520 | tf_op jit(solution)/shard_map/all_gather | solution.py:84
  233.8 10.7 %reduce_sum.62 = bf16[768,1408]{1,0:T(8,128)(2,1)} reduce(bf16[8,768,1408]{2,1,0:T(8,128)(2,1)} %bitcast.74, bf16[]{:T(256)} %constant.45.clone.1), dimensions={0}, to_apply=%region_7.8 | reduce | flops 7569408 | bytes 19464194 | tf_op jit(solution)/shard_map/reduce_sum | solution.py:84
  244.5 109.7 %all-reduce.6.cloned.1.call-done = (bf16[768,1408]{1,0:T(8,128)(2,1)}, bf16[768,1408]{1,0:T(8,128)(2,1)}) async-done(((bf16[768,1408]{1,0:T(8,128)(2,1)}, bf16[768,1408]{1,0:T(8,128)(2,1)}), (bf16[768,1408]{1,0:T(8,128)(2,1)}, bf16[768,1408]{1,0:T(8,128)(2,1)})) %all-reduce.6.cloned.1.call-update) | async-done | bytes 4325392 | tf_op jit(solution)/shard_map/psum | solution.py:86
  354.2 6.4 fusion.3
  360.6 2.3 fusion.21
  362.9 7.5 %all-to-all-start.1 = ((bf16[32,24,512]{2,1,0:T(8,128)(2,1)}), bf16[32,24,512]{2,1,0:T(8,128)(2,1)S(1)}, u32[]{:S(2)}, u32[]{:S(2)}) async-start(bf16[32,24,512]{2,1,0:T(8,128)(2,1)} %bitcast.9), calls=%async_computation.1 | async-start | bytes 1572864 | tf_op jit(solution)/shard_map/all_to_all | solution.py:102
  370.4 0.8 convert_element_type.130
  371.3 3.5 fusion.15
  374.8 2.2 add_convert_fusion
  377.1 6.4 all-to-all-done.1
  383.5 4.7 all-to-all-start.4
  388.2 0.0 all-reduce.4.cloned.1.call-start
  388.3 4.4 fusion.8
  392.6 2.4 fusion.9
  395.1 2.5 fusion.10
  397.6 2.6 gather_fusion.1
  400.2 2.7 reshape.149
  402.9 4.0 multiply_reduce_fusion
  406.9 0.1 copy.60
  407.0 13.9 %psum.38 = f32[256,2]{0,1:T(2,128)S(1)} all-reduce(f32[256,2]{0,1:T(2,128)S(1)} %copy.60), channel_id=1, replica_groups=mesh['ctx'=32,'head'=8] {'head'}, use_global_device_ids=true, to_apply=%region_11.12 | all-reduce | flops 512 | bytes 4096 | tf_op jit(solution)/shard_map/psum | solution.py:129
  420.9 2.0 gather_fusion.4
  422.9 0.2 reshape.148
  423.1 0.7 fusion.36
  423.9 0.9 convolution_bitcast_fusion
  424.8 1.1 fusion.26
  425.9 283.0 %all-reduce.4.cloned.1.call-done = f32[512,32]{0,1:T(8,128)} async-done(((f32[512,32]{0,1:T(8,128)}), f32[512,32]{0,1:T(8,128)}) %all-reduce.4.cloned.1.call-update) | async-done | bytes 65552 | tf_op jit(solution)/shard_map/psum | solution.py:140
  709.0 1.5 copy.70
  (57 shorter events, 0.3 us)
Async XLA Ops:
  7.2 83.2 %copy-start = (bf16[1,1408,512]{2,1,0:T(8,128)(2,1)S(1)}, bf16[1,1408,512]{2,1,0:T(8,128)(2,1)}, u32[]{:S(2)}) copy-start(bf16[1,1408,512]{2,1,0:T(8,128)(2,1)} %param.13) | copy-start | bytes 4325380
  7.2 6.4 copy-start.2
  7.2 226.6 %all-gather.3.cloned.1.call-start = ((), (), s32[]{:S(2)}) async-start(), calls=%async_computation.6 | async-start | bytes 19464192 | tf_op jit(solution)/shard_map/all_gather | solution.py:84
  11.0 2.5 copy-start.18
  13.5 2.7 copy-start.1
  16.3 3.6 copy-start.13
  36.5 0.5 copy-start.16
  36.5 1.1 copy-start.14
  48.9 22.0 %copy-start.20 = (bf16[1,1408,512]{2,1,0:T(8,128)(2,1)S(1)}, bf16[1,1408,512]{2,1,0:T(8,128)(2,1)}, u32[]{:S(2)}) copy-start(bf16[1,1408,512]{2,1,0:T(8,128)(2,1)} %param.12) | copy-start | bytes 4325380
  70.9 7.3 %copy-start.8 = (bf16[32,24,512]{2,1,0:T(8,128)(2,1)}, bf16[32,24,512]{2,1,0:T(8,128)(2,1)S(1)}, u32[]{:S(2)}) copy-start(bf16[32,24,512]{2,1,0:T(8,128)(2,1)S(1)} %all_to_all.26) | copy-start | bytes 2359300
  73.7 16.6 %all-to-all-start.3 = ((bf16[32,24,512]{2,1,0:T(8,128)(2,1)}), bf16[32,24,512]{2,1,0:T(8,128)(2,1)S(1)}, u32[]{:S(2)}, u32[]{:S(2)}) async-start(bf16[32,24,512]{2,1,0:T(8,128)(2,1)} %get-tuple-element.19), calls=%async_computation.3 | async-start | bytes 1572864 | tf_op jit(solution)/shard_map/all_to_all | solution.py:69
  78.1 276.1 %all-reduce.6.cloned.1.call-start = ((), (), s32[]{:S(2)}) async-start(), calls=%async_computation.7 | async-start | bytes 8650752 | tf_op jit(solution)/shard_map/psum | solution.py:86
  90.3 2.8 copy-start.10
  360.6 2.3 copy-start.3
  362.9 8.3 %copy-start.19 = (s32[512,1]{0,1:T(1,128)S(1)}, s32[512,1]{0,1:T(1,128)}, u32[]{:S(2)}) copy-start(s32[512,1]{0,1:T(1,128)} %copy-done.18) | copy-start | bytes 6148
  362.9 20.6 %all-to-all-start.1 = ((bf16[32,24,512]{2,1,0:T(8,128)(2,1)}), bf16[32,24,512]{2,1,0:T(8,128)(2,1)S(1)}, u32[]{:S(2)}, u32[]{:S(2)}) async-start(bf16[32,24,512]{2,1,0:T(8,128)(2,1)} %bitcast.9), calls=%async_computation.1 | async-start | bytes 1572864 | tf_op jit(solution)/shard_map/all_to_all | solution.py:102
  371.3 3.6 copy-start.6
  371.3 3.6 copy-start.21
  383.5 37.4 %all-to-all-start.4 = ((bf16[32,24,512]{2,1,0:T(8,128)(2,1)}), bf16[32,24,512]{2,1,0:T(8,128)(2,1)S(1)}, u32[]{:S(2)}, u32[]{:S(2)}) async-start(bf16[32,24,512]{2,1,0:T(8,128)(2,1)} %bitcast.83), calls=%async_computation.4 | async-start | bytes 1572864 | tf_op jit(solution)/shard_map/all_to_all | solution.py:109
  388.2 320.8 %all-reduce.4.cloned.1.call-start = ((), (), s32[]{:S(2)}) async-start(), calls=%async_computation.5 | async-start | bytes 131072 | tf_op jit(solution)/shard_map/psum | solution.py:140
  388.2 4.4 copy-start.5
  388.2 4.4 copy-start.9
  392.6 2.5 copy-start.4
  392.6 2.4 copy-start.11
  397.6 5.3 copy-start.7
  400.2 20.6 %copy-start.15 = (f32[256,1]{0,1:T(1,128)S(1)}, f32[256,1]{0,1:T(1,128)}, u32[]{:S(2)}) copy-start(f32[256,1]{0,1:T(1,128)} %copy-done.14) | copy-start | bytes 3076
  400.2 20.6 %copy-start.17 = (f32[256,1]{0,1:T(1,128)S(1)}, f32[256,1]{0,1:T(1,128)}, u32[]{:S(2)}) copy-start(f32[256,1]{0,1:T(1,128)} %copy-done.16) | copy-start | bytes 3076
  422.9 1.9 copy-start.12
Sparse Core Ops, SparseCore 0:
  73.9 159.9 all-gather.2
  236.5 117.6 all-reduce.5
  424.9 284.0 all-reduce.3
